TPU v7x, 32 devices: a whole 2x2x4 slice. The times are simulated.
32 devices in a mesh: tm: 8 (over z, x), state: 4 (over y, core).
Axes of the slice: x: 2, y: 2, z: 4, core: 2. Of those that a mesh axis runs over, the one named last changes fastest.
Arguments:
- obs: bfloat16 [2048, 16, 256], P(('state', 'tm')), may hold values from -6 to 6
- mask: int32 [2048, 16], P(('state', 'tm')), may hold values 0 or 1
- loadings: bfloat16 [2048, 2048], P('state'), may hold values from -0.125 to 0.125
- decay: float32 [16, 2048], P('tm', 'state'), may hold values from 0 to 1, as said below
Outputs:
- smoothed: float32 [2048, 16, 256], P('state', 'tm')
- residual: float32 [2048, 16, 256], P('state', 'tm')
Inputs may be any that keep to these rules, and one draw needn't show every extreme that they name: Every decay lies strictly between 0 and 1.
All inputs are finite; a program needn't handle non-finite values. No bound on the sum of `mask` on one device may be relied on, other than what follows from the above.
Results may differ from a plain program's by a relative error of at most 0.0021.
Values may be sent and summed in bfloat16 or wider, within the bound.
No kernel may reach another device: no remote copies, remote signals or barrier semaphores. Data moves between devices by JAX's collectives and lax.ppermute only.
A program may use at most 64 MiB of HBM per device.

v0:
```python
import jax
import jax.numpy as jnp
from jax import lax
from jax.sharding import PartitionSpec as P

CHUNKS = 2


def smooth_chunk(information, decay_all):
    comps, hours, width = information.shape
    state = jnp.zeros((comps, width), jnp.float32)
    filtered = []
    for hour in range(hours):
        state = decay_all[hour][:, None] * state + information[:, hour, :]
        filtered.append(state)
    state = jnp.zeros((comps, width), jnp.float32)
    rows = [None] * hours
    for hour in reversed(range(hours)):
        rate = decay_all[hour]
        state = rate[:, None] * state + (1.0 - rate * rate)[:, None] * filtered[hour]
        rows[hour] = state
    return jnp.stack(rows, axis=1)


def local(obs, mask, loadings, decay):
    tm_count = lax.axis_size("tm")
    tm_index = lax.axis_index("tm")
    _, hours, members = obs.shape
    chunk_members = members // CHUNKS
    masked = obs * mask[:, :, None].astype(obs.dtype)
    by_hour = lax.all_to_all(masked, "tm", split_axis=1, concat_axis=0, tiled=True)
    slab_hours, comps = decay.shape
    padded = jnp.zeros((tm_count, slab_hours, comps), jnp.float32)
    padded = lax.dynamic_update_slice(padded, decay[None], (tm_index, 0, 0))
    decay_all = lax.psum(padded, "tm").reshape(tm_count * slab_hours, comps)
    smoothed_parts = []
    residual_parts = []
    for chunk in range(CHUNKS):
        low = chunk * chunk_members
        piece = masked[:, :, low : low + chunk_members]
        by_member = lax.all_to_all(piece, "tm", split_axis=2, concat_axis=0, tiled=True)
        stations_here, _, width = by_member.shape
        partial = jnp.dot(
            loadings.T,
            by_member.reshape(stations_here, hours * width),
            preferred_element_type=jnp.float32,
        )
        information = lax.psum_scatter(partial, "state", scatter_dimension=0, tiled=True)
        information = information.reshape(information.shape[0], hours, width)
        smoothed_here = smooth_chunk(information, decay_all)
        smoothed = lax.all_to_all(smoothed_here, "tm", split_axis=1, concat_axis=2, tiled=True)
        rounded = smoothed.astype(jnp.bfloat16)
        fitted = jnp.einsum(
            "so,ogy->sgy",
            loadings,
            lax.all_gather(rounded, "state", axis=0, tiled=True),
            preferred_element_type=jnp.float32,
        )
        residual = by_hour[:, :, low : low + chunk_members].astype(jnp.float32) - fitted
        smoothed_parts.append(smoothed)
        residual_parts.append(residual)
    return (jnp.concatenate(smoothed_parts, axis=2), jnp.concatenate(residual_parts, axis=2))


def solution(mesh):
    return jax.shard_map(
        local,
        mesh=mesh,
        in_specs=(
            P(("state", "tm"), None, None),
            P(("state", "tm"), None),
            P("state", None),
            P("tm", "state"),
        ),
        out_specs=(P("state", "tm", None), P("state", "tm", None)),
        check_vma=False,
    )
```

profile of v0, /device:TPU:0, one launch (start us, length us, event | category | flops | bytes accessed | tf_op | source)
XLA Modules:
  0.0 196.1 jit_solution(5214605081453235125)
XLA Ops:
  8.1 3.5 %copy.34 = bf16[64,16,256]{0,1,2:T(8,128)(2,1)} copy(bf16[64,16,256]{2,1,0:T(8,128)(2,1)} %param.4) | data formatting | bytes 1048576 | tf_op args[0]
  14.0 1.4 reshape.7069
  15.5 16.1 %all_to_all.84 = bf16[8,2,8192]{2,1,0:T(2,128)(2,1)} all-to-all(bf16[8,2,8192]{2,1,0:T(2,128)(2,1)S(1)} %reshape.7069), channel_id=1, replica_groups=mesh['tm'=8,'state'=4] {'tm'}, dimensions={0} | all-to-all | bytes 524288 | tf_op jit(solution)/shard_map/all_to_all | solution.py:41
  31.6 2.1 %reshape.7070 = bf16[128,16,64]{2,1,0:T(8,128)(2,1)} reshape(bf16[8,2,8192]{2,1,0:T(2,128)(2,1)} %all_to_all.84) | data formatting | bytes 524288
  33.7 2.2 %copy.39 = bf16[8,64,16,16]{1,0,3,2:T(8,128)(2,1)} copy(bf16[8,64,16,16]{1,2,3,0:T(8,128)(2,1)} %bitcast.86) | data formatting | bytes 524288 | tf_op jit(solution)/shard_map/all_to_all | solution.py:41
  37.2 2.0 %convolution_bitcast_fusion = f32[2048,256]{0,1:T(8,128)} fusion(bf16[512,256]{0,1:T(8,128)(2,1)S(1)} %reshape.7066, bf16[512,2048]{1,0:T(8,128)(2,1)S(1)} %copy-done), kind=kOutput, calls=%fused_computation | convolution fusion | flops 536870912 | bytes 4456448 | tf_op jit(solution)/shard_map/dot_general | solution.py:43
  39.4 1.4 reshape.7071
  40.8 12.1 %all_to_all.85 = bf16[8,2,8192]{2,1,0:T(2,128)(2,1)} all-to-all(bf16[8,2,8192]{2,1,0:T(2,128)(2,1)S(1)} %reshape.7071), channel_id=1, replica_groups=mesh['tm'=8,'state'=4] {'tm'}, dimensions={0} | all-to-all | bytes 524288 | tf_op jit(solution)/shard_map/all_to_all | solution.py:41
  52.8 2.1 %reshape.7072 = bf16[128,16,64]{2,1,0:T(8,128)(2,1)} reshape(bf16[8,2,8192]{2,1,0:T(2,128)(2,1)} %all_to_all.85) | data formatting | bytes 524288
  55.0 2.3 %copy.36 = bf16[8,64,16,16]{1,0,3,2:T(8,128)(2,1)} copy(bf16[8,64,16,16]{1,2,3,0:T(8,128)(2,1)} %bitcast.87) | data formatting | bytes 524288 | tf_op jit(solution)/shard_map/all_to_all | solution.py:41
  58.6 2.1 %convolution_bitcast_fusion.1 = f32[2048,256]{0,1:T(8,128)} fusion(bf16[512,256]{0,1:T(8,128)(2,1)S(1)} %reshape.7064, bf16[512,2048]{1,0:T(8,128)(2,1)S(1)} %copy-done), kind=kOutput, calls=%fused_computation.1 | convolution fusion | flops 536870912 | bytes 4456448 | tf_op jit(solution)/shard_map/dot_general | solution.py:43
  61.4 35.2 %psum.7 = f32[16,512]{1,0:T(8,128)S(1)} all-reduce(f32[16,512]{1,0:T(8,128)S(1)} %reshape.7063), channel_id=1, replica_groups=mesh['tm'=8,'state'=4] {'tm'}, use_global_device_ids=true, to_apply=%region_0.0 | all-reduce | flops 8192 | bytes 65536 | tf_op jit(solution)/shard_map/psum | solution.py:35
  101.6 1.9 constant_dynamic-update-slice_fusion.31
  117.0 1.5 constant_dynamic-update-slice_fusion
  118.5 20.1 %all_to_all.86 = f32[512,16,16]{0,2,1:T(8,128)S(1)} all-to-all(f32[512,16,16]{0,2,1:T(8,128)} %get-tuple-element.61), channel_id=1, replica_groups=mesh['tm'=8,'state'=4] {'tm'}, dimensions={1} | all-to-all | bytes 1048576 | tf_op jit(solution)/shard_map/all_to_all | solution.py:51
  140.2 4.2 %all-to-all-start.1 = ((f32[512,16,16]{0,2,1:T(8,128)}), f32[512,16,16]{0,2,1:T(8,128)}, u32[]{:S(2)}, u32[]{:S(2)}) async-start(f32[512,16,16]{0,2,1:T(8,128)} %copy-done.3), calls=%async_computation.2 | async-start | bytes 1048576 | tf_op jit(solution)/shard_map/all_to_all | solution.py:51
  144.3 1.6 copy.41
  146.0 12.1 %all-to-all-done.1 = f32[512,16,16]{0,2,1:T(8,128)} async-done(((f32[512,16,16]{0,2,1:T(8,128)}), f32[512,16,16]{0,2,1:T(8,128)}, u32[]{:S(2)}, u32[]{:S(2)}) %all-to-all-start.1) | async-done | bytes 524320 | tf_op jit(solution)/shard_map/all_to_all | solution.py:51
  158.0 4.1 %all-to-all-start.4 = ((bf16[64,16,256]{2,0,1:T(8,128)(2,1)}), bf16[64,16,256]{2,0,1:T(8,128)(2,1)}, u32[]{:S(2)}, u32[]{:S(2)}) async-start(bf16[64,16,256]{2,0,1:T(8,128)(2,1)} %copy.41), calls=%async_computation.6 | async-start | bytes 1048576 | tf_op jit(solution)/shard_map/all_to_all | solution.py:31
  164.1 11.4 %all-to-all-done.4 = bf16[64,16,256]{2,0,1:T(8,128)(2,1)} async-done(((bf16[64,16,256]{2,0,1:T(8,128)(2,1)}), bf16[64,16,256]{2,0,1:T(8,128)(2,1)}, u32[]{:S(2)}, u32[]{:S(2)}) %all-to-all-start.4) | async-done | bytes 524320 | tf_op jit(solution)/shard_map/all_to_all | solution.py:31
  177.4 1.8 copy.49
  181.1 2.2 %copy.45 = f32[512,2,256]{2,1,0:T(2,128)} copy(f32[512,2,256]{0,2,1:T(8,128)} %pad_maximum_fusion) | data formatting | bytes 2097152
  183.4 2.8 %fusion.13 = f32[512,2,128]{0,2,1:T(8,128)} fusion(bf16[2048,2,128]{0,2,1:T(8,128)(2,1)} %all-gather.5.cloned.1.call-done, bf16[512,2048]{1,0:T(8,128)(2,1)S(1)} %copy-done, bf16[512,2,128]{0,2,1:T(8,128)(2,1)S(1)} %copy-done.6), kind=kOutput, calls=%fused_computation.9 | convolution fusion | flops 537133056 | bytes 3932160 | tf_op jit(solution)/shard_map/so,ogy->sgy/dot_general | solution.py:53
  186.2 2.0 %fusion.7 = f32[512,2,128]{0,2,1:T(8,128)S(1)} fusion(bf16[2048,2,128]{0,2,1:T(8,128)(2,1)} %all-gather.3.cloned.1.call-done, bf16[512,2048]{1,0:T(8,128)(2,1)S(1)} %copy-done, bf16[512,2,128]{0,2,1:T(8,128)(2,1)S(1)} %copy-done.5), kind=kOutput, calls=%fused_computation.7 | convolution fusion | flops 537133056 | bytes 3932160 | tf_op jit(solution)/shard_map/so,ogy->sgy/dot_general | solution.py:53
  (111 shorter events, 33.7 us)
Async XLA Ops:
  7.2 30.1 %copy-start = (bf16[512,2048]{1,0:T(8,128)(2,1)S(1)}, bf16[512,2048]{1,0:T(8,128)(2,1)}, u32[]{:S(2)}) copy-start(bf16[512,2048]{1,0:T(8,128)(2,1)} %param.6) | copy-start | bytes 6291460
  7.2 94.3 %reduce-scatter.5.cloned.1.call-start = ((), (), s32[]{:S(2)}) async-start(), calls=%async_computation.8 | async-start | bytes 2621440 | tf_op jit(solution)/shard_map/reduce_scatter | solution.py:48
  39.3 64.7 %reduce-scatter.3.cloned.1.call-start = ((), (), s32[]{:S(2)}) async-start(), calls=%async_computation.7 | async-start | bytes 2621440 | tf_op jit(solution)/shard_map/reduce_scatter | solution.py:48
  60.7 122.6 %all-gather.5.cloned.1.call-start = ((), (), s32[]{:S(2)}) async-start(), calls=%async_computation.10 | async-start | bytes 1310720 | tf_op jit(solution)/shard_map/all_gather | solution.py:56
  96.6 4.9 %copy-start.7 = (f32[1,512]{1,0:T(1,128)}, f32[1,512]{1,0:T(1,128)S(1)}, u32[]{:S(2)}) copy-start(f32[1,512]{1,0:T(1,128)S(1)} %get-tuple-element.50) | copy-start | bytes 6148
  96.6 4.9 %copy-start.9 = (f32[1,512]{1,0:T(1,128)}, f32[1,512]{1,0:T(1,128)S(1)}, u32[]{:S(2)}) copy-start(f32[1,512]{1,0:T(1,128)S(1)} %get-tuple-element.52) | copy-start | bytes 6148
  96.6 4.9 %copy-start.11 = (f32[1,512]{1,0:T(1,128)}, f32[1,512]{1,0:T(1,128)S(1)}, u32[]{:S(2)}) copy-start(f32[1,512]{1,0:T(1,128)S(1)} %get-tuple-element.54) | copy-start | bytes 6148
  96.7 4.9 %copy-start.12 = (f32[1,512]{1,0:T(1,128)}, f32[1,512]{1,0:T(1,128)S(1)}, u32[]{:S(2)}) copy-start(f32[1,512]{1,0:T(1,128)S(1)} %get-tuple-element.56) | copy-start | bytes 6148
  96.7 4.9 %copy-start.13 = (f32[1,512]{1,0:T(1,128)}, f32[1,512]{1,0:T(1,128)S(1)}, u32[]{:S(2)}) copy-start(f32[1,512]{1,0:T(1,128)S(1)} %get-tuple-element.58) | copy-start | bytes 6148
  96.7 4.9 %copy-start.17 = (f32[1,512]{1,0:T(1,128)}, f32[1,512]{1,0:T(1,128)S(1)}, u32[]{:S(2)}) copy-start(f32[1,512]{1,0:T(1,128)S(1)} %get-tuple-element.47) | copy-start | bytes 6148
  96.7 4.9 %copy-start.18 = (f32[1,512]{1,0:T(1,128)}, f32[1,512]{1,0:T(1,128)S(1)}, u32[]{:S(2)}) copy-start(f32[1,512]{1,0:T(1,128)S(1)} %get-tuple-element.49) | copy-start | bytes 6148
  96.7 4.9 %copy-start.19 = (f32[1,512]{1,0:T(1,128)}, f32[1,512]{1,0:T(1,128)S(1)}, u32[]{:S(2)}) copy-start(f32[1,512]{1,0:T(1,128)S(1)} %get-tuple-element.51) | copy-start | bytes 6148
  96.7 4.9 %copy-start.20 = (f32[1,512]{1,0:T(1,128)}, f32[1,512]{1,0:T(1,128)S(1)}, u32[]{:S(2)}) copy-start(f32[1,512]{1,0:T(1,128)S(1)} %get-tuple-element.53) | copy-start | bytes 6148
  96.7 4.9 %copy-start.21 = (f32[1,512]{1,0:T(1,128)}, f32[1,512]{1,0:T(1,128)S(1)}, u32[]{:S(2)}) copy-start(f32[1,512]{1,0:T(1,128)S(1)} %get-tuple-element.55) | copy-start | bytes 6148
  104.0 7.3 %copy-start.10 = (f32[1,512]{1,0:T(1,128)S(1)}, f32[1,512]{1,0:T(1,128)}, u32[]{:S(2)}) copy-start(f32[1,512]{1,0:T(1,128)} %copy-done.9) | copy-start | bytes 6148
  104.0 7.3 %copy-start.16 = (f32[512]{0:T(512)S(1)}, f32[512]{0:T(512)}, u32[]{:S(2)}) copy-start(f32[512]{0:T(512)} %get-tuple-element.86) | copy-start | bytes 6148
  104.0 8.6 %copy-start.8 = (f32[1,512]{1,0:T(1,128)S(1)}, f32[1,512]{1,0:T(1,128)}, u32[]{:S(2)}) copy-start(f32[1,512]{1,0:T(1,128)} %copy-done.7) | copy-start | bytes 6148
  104.0 8.6 %copy-start.15 = (f32[512]{0:T(512)S(1)}, f32[512]{0:T(512)}, u32[]{:S(2)}) copy-start(f32[512]{0:T(512)} %get-tuple-element.88) | copy-start | bytes 6148
  104.0 9.8 %copy-start.14 = (f32[512]{0:T(512)S(1)}, f32[512]{0:T(512)}, u32[]{:S(2)}) copy-start(f32[512]{0:T(512)} %get-tuple-element.90) | copy-start | bytes 6148
  118.5 20.1 %copy-start.3 = (f32[512,16,16]{0,2,1:T(8,128)}, f32[512,16,16]{0,2,1:T(8,128)S(1)}, u32[]{:S(2)}) copy-start(f32[512,16,16]{0,2,1:T(8,128)S(1)} %get-tuple-element.60) | copy-start | bytes 1572868
  140.2 17.9 %all-to-all-start.1 = ((f32[512,16,16]{0,2,1:T(8,128)}), f32[512,16,16]{0,2,1:T(8,128)}, u32[]{:S(2)}, u32[]{:S(2)}) async-start(f32[512,16,16]{0,2,1:T(8,128)} %copy-done.3), calls=%async_computation.2 | async-start | bytes 1048576 | tf_op jit(solution)/shard_map/all_to_all | solution.py:51
  158.0 17.5 %all-to-all-start.4 = ((bf16[64,16,256]{2,0,1:T(8,128)(2,1)}), bf16[64,16,256]{2,0,1:T(8,128)(2,1)}, u32[]{:S(2)}, u32[]{:S(2)}) async-start(bf16[64,16,256]{2,0,1:T(8,128)(2,1)} %copy.41), calls=%async_computation.6 | async-start | bytes 1048576 | tf_op jit(solution)/shard_map/all_to_all | solution.py:31
  162.2 24.0 %all-gather.3.cloned.1.call-start = ((), (), s32[]{:S(2)}) async-start(), calls=%async_computation.9 | async-start | bytes 1310720 | tf_op jit(solution)/shard_map/all_gather | solution.py:56
  163.3 16.7 %copy-start.2 = (f32[512,8,2,16]{0,3,1,2:T(8,128)S(1)}, f32[512,8,2,16]{0,3,1,2:T(8,128)}, u32[]{:S(2)}) copy-start(f32[512,8,2,16]{0,3,1,2:T(8,128)} %copy-done.1) | copy-start | bytes 1572868
  (7 other events, 19.4 us)
Sparse Core Ops, SparseCore 0:
  39.4 30.4 reduce-scatter.4
  72.6 31.3 reduce-scatter.2
  140.3 14.7 all-gather.4
  164.3 17.0 all-gather.2
where the time goes:
time: 198 us; the launch traced here: 196 us
  blocking collectives  83.4 us (42%)
  local copies, waits for them, and re-layouts  35.7 us (18%)
  waiting for transfers between devices  24.1 us (12%)
  other arithmetic  21.4 us (11%)
  between operations  14.1 us (7%)
  matrix products  8.94 us (5%)
  starting transfers between devices  8.46 us (4%)
    psum x1, blocking collectives, local(): decay_all = lax.psum(padded, 'tm').reshape(tm_count * slab_hours, comps)  35.2 us
    all_to_all x2, blocking collectives, local(): lax.all_to_all(piece, 'tm', split_axis=2, concat_axis=0, tiled=True)  28.1 us
    unnamed x73, local copies, waits for them, and re-layouts  22.7 us
    all_to_all x1, blocking collectives, local(): lax.all_to_all(smoothed_here, 'tm', split_axis=1, concat_axis=2, tiled=True)  20.1 us
    all_to_all x1, waiting for transfers between devices, local(): lax.all_to_all(smoothed_here, 'tm', split_axis=1, concat_axis=2, tiled=True)  12.1 us
    all_to_all x1, waiting for transfers between devices, local(): lax.all_to_all(masked, 'tm', split_axis=1, concat_axis=0, tiled=True)  11.4 us
    unnamed x9, other arithmetic  10.5 us
    dot_general x2, matrix products, local(): jnp.einsum('so,ogy->sgy', loadings, lax.all_gather(rounded, 'state', axis...  4.83 us
  transfers between devices with their start and end apart: 6, of which 3 were waited for; matrix products, arithmetic and copies ran while one was open for 15% of the time, Pallas kernels for 0%

commit v1 on v0

--- a/solution.py
+++ b/solution.py
@@ -4,6 +4,11 @@
 from jax.sharding import PartitionSpec as P
 
 CHUNKS = 2
+
+
+def summed_here(x, mesh_axis):
+    pieces = lax.all_gather(x, mesh_axis)
+    return jnp.sum(pieces, axis=0)
 
 
 def smooth_chunk(information, decay_all):
@@ -32,7 +37,7 @@
     slab_hours, comps = decay.shape
     padded = jnp.zeros((tm_count, slab_hours, comps), jnp.float32)
     padded = lax.dynamic_update_slice(padded, decay[None], (tm_index, 0, 0))
-    decay_all = lax.psum(padded, "tm").reshape(tm_count * slab_hours, comps)
+    decay_all = summed_here(padded, "tm").reshape(tm_count * slab_hours, comps)
     smoothed_parts = []
     residual_parts = []
     for chunk in range(CHUNKS):

time: 198 us -> 198 us (level)
  blocking collectives: 83.4 us -> 79 us
  waiting for transfers between devices: 24.1 us -> 28.3 us
    psum x1 -> x0, blocking collectives: 35.2 us -> none  [local(): decay_all = lax.psum(padded, 'tm').reshape(tm_count * slab_hours, comps)]
    all_gather x0 -> x1, blocking collectives: none -> 30.8 us  [summed_here(): pieces = lax.all_gather(x, mesh_axis)]
    reduce_scatter x2, waiting for transfers between devices: 0.49 us -> 4.73 us  [local(): lax.psum_scatter(partial, 'state', scatter_dimension=0, tiled=True)]
where the time goes in v1:
time: 198 us; the launch traced here: 196 us
  blocking collectives  79 us (40%)
  local copies, waits for them, and re-layouts  35.8 us (18%)
  waiting for transfers between devices  28.3 us (14%)
  other arithmetic  21.5 us (11%)
  between operations  14.1 us (7%)
  matrix products  8.94 us (5%)
  starting transfers between devices  8.46 us (4%)
    all_gather x1, blocking collectives, summed_here(): pieces = lax.all_gather(x, mesh_axis)  30.8 us
    all_to_all x2, blocking collectives, local(): lax.all_to_all(piece, 'tm', split_axis=2, concat_axis=0, tiled=True)  28.1 us
    unnamed x73, local copies, waits for them, and re-layouts  22.7 us
    all_to_all x1, blocking collectives, local(): lax.all_to_all(smoothed_here, 'tm', split_axis=1, concat_axis=2, tiled=True)  20.1 us
    all_to_all x1, waiting for transfers between devices, local(): lax.all_to_all(smoothed_here, 'tm', split_axis=1, concat_axis=2, tiled=True)  12.1 us
    all_to_all x1, waiting for transfers between devices, local(): lax.all_to_all(masked, 'tm', split_axis=1, concat_axis=0, tiled=True)  11.4 us
    unnamed x9, other arithmetic  10.5 us
    dot_general x2, matrix products, local(): jnp.einsum('so,ogy->sgy', loadings, lax.all_gather(rounded, 'state', axis...  4.83 us
  transfers between devices with their start and end apart: 6, of which 3 were waited for; matrix products, arithmetic and copies ran while one was open for 15% of the time, Pallas kernels for 0%

profile of v1, /device:TPU:0, one launch (start us, length us, event | category | flops | bytes accessed | tf_op | source)
XLA Modules:
  0.0 196.1 jit_solution(8259506804306454687)
XLA Ops:
  8.1 3.5 %copy.61 = bf16[64,16,256]{0,1,2:T(8,128)(2,1)} copy(bf16[64,16,256]{2,1,0:T(8,128)(2,1)} %param.4) | data formatting | bytes 1048576 | tf_op args[0]
  15.5 16.1 %all_to_all.84 = bf16[8,2,8192]{2,1,0:T(2,128)(2,1)} all-to-all(bf16[8,2,8192]{2,1,0:T(2,128)(2,1)S(1)} %reshape.7072), channel_id=1, replica_groups=mesh['tm'=8,'state'=4] {'tm'}, dimensions={0} | all-to-all | bytes 524288 | tf_op jit(solution)/shard_map/all_to_all | solution.py:46
  31.6 2.1 %reshape.7073 = bf16[128,16,64]{2,1,0:T(8,128)(2,1)} reshape(bf16[8,2,8192]{2,1,0:T(2,128)(2,1)} %all_to_all.84) | data formatting | bytes 524288
  33.7 2.2 %copy.66 = bf16[8,64,16,16]{1,0,3,2:T(8,128)(2,1)} copy(bf16[8,64,16,16]{1,2,3,0:T(8,128)(2,1)} %bitcast.84) | data formatting | bytes 524288 | tf_op jit(solution)/shard_map/all_to_all | solution.py:46
  37.2 2.0 %convolution_bitcast_fusion = f32[2048,256]{0,1:T(8,128)} fusion(bf16[512,256]{0,1:T(8,128)(2,1)S(1)} %reshape.7069, bf16[512,2048]{1,0:T(8,128)(2,1)S(1)} %copy-done), kind=kOutput, calls=%fused_computation | convolution fusion | flops 536870912 | bytes 4456448 | tf_op jit(solution)/shard_map/dot_general | solution.py:48
  39.4 1.4 reshape.7074
  40.8 12.1 %all_to_all.85 = bf16[8,2,8192]{2,1,0:T(2,128)(2,1)} all-to-all(bf16[8,2,8192]{2,1,0:T(2,128)(2,1)S(1)} %reshape.7074), channel_id=1, replica_groups=mesh['tm'=8,'state'=4] {'tm'}, dimensions={0} | all-to-all | bytes 524288 | tf_op jit(solution)/shard_map/all_to_all | solution.py:46
  52.8 2.1 %reshape.7075 = bf16[128,16,64]{2,1,0:T(8,128)(2,1)} reshape(bf16[8,2,8192]{2,1,0:T(2,128)(2,1)} %all_to_all.85) | data formatting | bytes 524288
  55.0 2.3 %copy.63 = bf16[8,64,16,16]{1,0,3,2:T(8,128)(2,1)} copy(bf16[8,64,16,16]{1,2,3,0:T(8,128)(2,1)} %bitcast.85) | data formatting | bytes 524288 | tf_op jit(solution)/shard_map/all_to_all | solution.py:46
  58.6 2.1 %convolution_bitcast_fusion.1 = f32[2048,256]{0,1:T(8,128)} fusion(bf16[512,256]{0,1:T(8,128)(2,1)S(1)} %reshape.7067, bf16[512,2048]{1,0:T(8,128)(2,1)S(1)} %copy-done), kind=kOutput, calls=%fused_computation.1 | convolution fusion | flops 536870912 | bytes 4456448 | tf_op jit(solution)/shard_map/dot_general | solution.py:48
  61.5 30.8 %all_gather.13 = f32[8,8,2,512]{3,1,2,0:T(8,128)S(1)} all-gather(f32[1,8,2,512]{3,1,2,0:T(8,128)S(1)} %dynamic_update_slice.4), channel_id=1, replica_groups=mesh['tm'=8,'state'=4] {'tm'}, dimensions={0}, use_global_device_ids=true | all-gather | bytes 294912 | tf_op jit(solution)/shard_map/all_gather | solution.py:10
  97.4 1.9 constant_dynamic-update-slice_fusion.31
  99.3 4.7 %reduce-scatter.3.cloned.1.call-done = f32[512,256]{0,1:T(8,128)} async-done(((f32[2048,256]{0,1:T(8,128)}), f32[512,256]{0,1:T(8,128)}) %reduce-scatter.3.cloned.1.call-update) | async-done | bytes 524304 | tf_op jit(solution)/shard_map/reduce_scatter | solution.py:53
  117.0 1.5 constant_dynamic-update-slice_fusion
  118.5 20.1 %all_to_all.86 = f32[512,16,16]{0,2,1:T(8,128)S(1)} all-to-all(f32[512,16,16]{0,2,1:T(8,128)} %get-tuple-element.65), channel_id=1, replica_groups=mesh['tm'=8,'state'=4] {'tm'}, dimensions={1} | all-to-all | bytes 1048576 | tf_op jit(solution)/shard_map/all_to_all | solution.py:56
  140.2 4.2 %all-to-all-start.1 = ((f32[512,16,16]{0,2,1:T(8,128)}), f32[512,16,16]{0,2,1:T(8,128)}, u32[]{:S(2)}, u32[]{:S(2)}) async-start(f32[512,16,16]{0,2,1:T(8,128)} %copy-done.3), calls=%async_computation.2 | async-start | bytes 1048576 | tf_op jit(solution)/shard_map/all_to_all | solution.py:56
  144.3 1.6 copy.68
  146.0 12.1 %all-to-all-done.1 = f32[512,16,16]{0,2,1:T(8,128)} async-done(((f32[512,16,16]{0,2,1:T(8,128)}), f32[512,16,16]{0,2,1:T(8,128)}, u32[]{:S(2)}, u32[]{:S(2)}) %all-to-all-start.1) | async-done | bytes 524320 | tf_op jit(solution)/shard_map/all_to_all | solution.py:56
  158.0 4.1 %all-to-all-start.4 = ((bf16[64,16,256]{2,0,1:T(8,128)(2,1)}), bf16[64,16,256]{2,0,1:T(8,128)(2,1)}, u32[]{:S(2)}, u32[]{:S(2)}) async-start(bf16[64,16,256]{2,0,1:T(8,128)(2,1)} %copy.68), calls=%async_computation.6 | async-start | bytes 1048576 | tf_op jit(solution)/shard_map/all_to_all | solution.py:36
  164.1 11.4 %all-to-all-done.4 = bf16[64,16,256]{2,0,1:T(8,128)(2,1)} async-done(((bf16[64,16,256]{2,0,1:T(8,128)(2,1)}), bf16[64,16,256]{2,0,1:T(8,128)(2,1)}, u32[]{:S(2)}, u32[]{:S(2)}) %all-to-all-start.4) | async-done | bytes 524320 | tf_op jit(solution)/shard_map/all_to_all | solution.py:36
  177.4 1.8 copy.76
  181.1 2.2 %copy.72 = f32[512,2,256]{2,1,0:T(2,128)} copy(f32[512,2,256]{0,2,1:T(8,128)} %pad_maximum_fusion) | data formatting | bytes 2097152
  183.4 2.8 %fusion.13 = f32[512,2,128]{0,2,1:T(8,128)} fusion(bf16[2048,2,128]{0,2,1:T(8,128)(2,1)} %all-gather.5.cloned.1.call-done, bf16[512,2048]{1,0:T(8,128)(2,1)S(1)} %copy-done, bf16[512,2,128]{0,2,1:T(8,128)(2,1)S(1)} %copy-done.6), kind=kOutput, calls=%fused_computation.9 | convolution fusion | flops 537133056 | bytes 3932160 | tf_op jit(solution)/shard_map/so,ogy->sgy/dot_general | solution.py:58
  186.2 2.0 %fusion.7 = f32[512,2,128]{0,2,1:T(8,128)S(1)} fusion(bf16[2048,2,128]{0,2,1:T(8,128)(2,1)} %all-gather.3.cloned.1.call-done, bf16[512,2048]{1,0:T(8,128)(2,1)S(1)} %copy-done, bf16[512,2,128]{0,2,1:T(8,128)(2,1)S(1)} %copy-done.5), kind=kOutput, calls=%fused_computation.7 | convolution fusion | flops 537133056 | bytes 3932160 | tf_op jit(solution)/shard_map/so,ogy->sgy/dot_general | solution.py:58
  (114 shorter events, 34.8 us)
Async XLA Ops:
  7.2 30.1 %copy-start = (bf16[512,2048]{1,0:T(8,128)(2,1)S(1)}, bf16[512,2048]{1,0:T(8,128)(2,1)}, u32[]{:S(2)}) copy-start(bf16[512,2048]{1,0:T(8,128)(2,1)} %param.6) | copy-start | bytes 6291460
  7.2 90.1 %reduce-scatter.5.cloned.1.call-start = ((), (), s32[]{:S(2)}) async-start(), calls=%async_computation.8 | async-start | bytes 2621440 | tf_op jit(solution)/shard_map/reduce_scatter | solution.py:53
  39.3 64.7 %reduce-scatter.3.cloned.1.call-start = ((), (), s32[]{:S(2)}) async-start(), calls=%async_computation.7 | async-start | bytes 2621440 | tf_op jit(solution)/shard_map/reduce_scatter | solution.py:53
  60.7 122.6 %all-gather.5.cloned.1.call-start = ((), (), s32[]{:S(2)}) async-start(), calls=%async_computation.10 | async-start | bytes 1310720 | tf_op jit(solution)/shard_map/all_gather | solution.py:61
  92.4 4.9 %copy-start.7 = (f32[1,512]{1,0:T(1,128)}, f32[1,512]{1,0:T(1,128)S(1)}, u32[]{:S(2)}) copy-start(f32[1,512]{1,0:T(1,128)S(1)} %get-tuple-element.54) | copy-start | bytes 6148
  92.4 4.9 %copy-start.9 = (f32[1,512]{1,0:T(1,128)}, f32[1,512]{1,0:T(1,128)S(1)}, u32[]{:S(2)}) copy-start(f32[1,512]{1,0:T(1,128)S(1)} %get-tuple-element.56) | copy-start | bytes 6148
  92.4 4.9 %copy-start.11 = (f32[1,512]{1,0:T(1,128)}, f32[1,512]{1,0:T(1,128)S(1)}, u32[]{:S(2)}) copy-start(f32[1,512]{1,0:T(1,128)S(1)} %get-tuple-element.58) | copy-start | bytes 6148
  92.4 4.9 %copy-start.12 = (f32[1,512]{1,0:T(1,128)}, f32[1,512]{1,0:T(1,128)S(1)}, u32[]{:S(2)}) copy-start(f32[1,512]{1,0:T(1,128)S(1)} %get-tuple-element.60) | copy-start | bytes 6148
  92.4 4.9 %copy-start.13 = (f32[1,512]{1,0:T(1,128)}, f32[1,512]{1,0:T(1,128)S(1)}, u32[]{:S(2)}) copy-start(f32[1,512]{1,0:T(1,128)S(1)} %get-tuple-element.62) | copy-start | bytes 6148
  92.4 4.9 %copy-start.17 = (f32[1,512]{1,0:T(1,128)}, f32[1,512]{1,0:T(1,128)S(1)}, u32[]{:S(2)}) copy-start(f32[1,512]{1,0:T(1,128)S(1)} %get-tuple-element.51) | copy-start | bytes 6148
  92.4 4.9 %copy-start.18 = (f32[1,512]{1,0:T(1,128)}, f32[1,512]{1,0:T(1,128)S(1)}, u32[]{:S(2)}) copy-start(f32[1,512]{1,0:T(1,128)S(1)} %get-tuple-element.53) | copy-start | bytes 6148
  92.5 4.9 %copy-start.19 = (f32[1,512]{1,0:T(1,128)}, f32[1,512]{1,0:T(1,128)S(1)}, u32[]{:S(2)}) copy-start(f32[1,512]{1,0:T(1,128)S(1)} %get-tuple-element.55) | copy-start | bytes 6148
  92.5 4.9 %copy-start.20 = (f32[1,512]{1,0:T(1,128)}, f32[1,512]{1,0:T(1,128)S(1)}, u32[]{:S(2)}) copy-start(f32[1,512]{1,0:T(1,128)S(1)} %get-tuple-element.57) | copy-start | bytes 6148
  92.5 4.9 %copy-start.21 = (f32[1,512]{1,0:T(1,128)}, f32[1,512]{1,0:T(1,128)S(1)}, u32[]{:S(2)}) copy-start(f32[1,512]{1,0:T(1,128)S(1)} %get-tuple-element.59) | copy-start | bytes 6148
  104.0 7.3 %copy-start.10 = (f32[1,512]{1,0:T(1,128)S(1)}, f32[1,512]{1,0:T(1,128)}, u32[]{:S(2)}) copy-start(f32[1,512]{1,0:T(1,128)} %copy-done.9) | copy-start | bytes 6148
  104.0 7.3 %copy-start.16 = (f32[512]{0:T(512)S(1)}, f32[512]{0:T(512)}, u32[]{:S(2)}) copy-start(f32[512]{0:T(512)} %get-tuple-element.90) | copy-start | bytes 6148
  104.0 8.6 %copy-start.8 = (f32[1,512]{1,0:T(1,128)S(1)}, f32[1,512]{1,0:T(1,128)}, u32[]{:S(2)}) copy-start(f32[1,512]{1,0:T(1,128)} %copy-done.7) | copy-start | bytes 6148
  104.0 8.6 %copy-start.15 = (f32[512]{0:T(512)S(1)}, f32[512]{0:T(512)}, u32[]{:S(2)}) copy-start(f32[512]{0:T(512)} %get-tuple-element.92) | copy-start | bytes 6148
  104.0 9.8 %copy-start.14 = (f32[512]{0:T(512)S(1)}, f32[512]{0:T(512)}, u32[]{:S(2)}) copy-start(f32[512]{0:T(512)} %get-tuple-element.94) | copy-start | bytes 6148
  118.5 20.1 %copy-start.3 = (f32[512,16,16]{0,2,1:T(8,128)}, f32[512,16,16]{0,2,1:T(8,128)S(1)}, u32[]{:S(2)}) copy-start(f32[512,16,16]{0,2,1:T(8,128)S(1)} %get-tuple-element.64) | copy-start | bytes 1572868
  140.2 17.9 %all-to-all-start.1 = ((f32[512,16,16]{0,2,1:T(8,128)}), f32[512,16,16]{0,2,1:T(8,128)}, u32[]{:S(2)}, u32[]{:S(2)}) async-start(f32[512,16,16]{0,2,1:T(8,128)} %copy-done.3), calls=%async_computation.2 | async-start | bytes 1048576 | tf_op jit(solution)/shard_map/all_to_all | solution.py:56
  158.0 17.5 %all-to-all-start.4 = ((bf16[64,16,256]{2,0,1:T(8,128)(2,1)}), bf16[64,16,256]{2,0,1:T(8,128)(2,1)}, u32[]{:S(2)}, u32[]{:S(2)}) async-start(bf16[64,16,256]{2,0,1:T(8,128)(2,1)} %copy.68), calls=%async_computation.6 | async-start | bytes 1048576 | tf_op jit(solution)/shard_map/all_to_all | solution.py:36
  162.2 24.0 %all-gather.3.cloned.1.call-start = ((), (), s32[]{:S(2)}) async-start(), calls=%async_computation.9 | async-start | bytes 1310720 | tf_op jit(solution)/shard_map/all_gather | solution.py:61
  163.3 16.7 %copy-start.2 = (f32[512,8,2,16]{0,3,1,2:T(8,128)S(1)}, f32[512,8,2,16]{0,3,1,2:T(8,128)}, u32[]{:S(2)}) copy-start(f32[512,8,2,16]{0,3,1,2:T(8,128)} %copy-done.1) | copy-start | bytes 1572868
  (7 other events, 19.4 us)
Sparse Core Ops, SparseCore 0:
  39.4 30.4 reduce-scatter.4
  72.6 31.3 reduce-scatter.2
  140.3 14.7 all-gather.4
  164.3 17.0 all-gather.2
